TPU v7x, 32 devices: a whole 2x2x4 slice. The times are simulated.
32 devices in a mesh: groups: 2 (over x), dp: 16 (over z, y, core).
Axes of the slice: x: 2, y: 2, z: 4, core: 2. Of those that a mesh axis runs over, the one named last changes fastest.
Arguments:
- layer_input: bfloat16 [8192, 8192], P(('groups', 'dp')), parts along dimension 0, may hold values from -6 to 6
- grad_values: bfloat16 [8192, 1024], P(('groups', 'dp')), parts along dimension 0, may hold values from -6 to 6
- base_weight: bfloat16 [8192, 1024], P('dp'), may hold values from -0.0625 to 0.0625
- tile_ids: int32 [32], P(('groups', 'dp')), parts along dimension 0, may hold values from 0 to 511, as said below
- tile_delta: bfloat16 [32, 128, 128], P(('groups', 'dp')), parts along dimension 0, may hold values from -0.1875 to 0.1875
Outputs:
- grad_input: bfloat16 [8192, 8192], P(('groups', 'dp')), parts along dimension 0
- grad_tiles: float32 [32, 128, 128], P(('groups', 'dp')), parts along dimension 0
There are 2 independent parts, one for each index of `groups`. A program takes and returns all parts, laid end to end along the dimension named above; an argument that names none is the same for every part. Nothing has to cross between parts.
Inputs may be any that keep to these rules, and one draw needn't show every extreme that they name: `tile_ids`: the 16 tile numbers are distinct; every tile of some tile row is listed.
All inputs are finite; a program needn't handle non-finite values.
Results may differ from a plain program's by a relative error of at most 0.0034.
Values may be sent and summed in bfloat16 or wider, within the bound.
No kernel may reach another device: no remote copies, remote signals or barrier semaphores. Data moves between devices by JAX's collectives and lax.ppermute only.
A program may use at most 128 MiB of HBM per device.

v0:
```python
import math
import jax
import jax.numpy as jnp
from jax import lax
from jax.sharding import PartitionSpec as P

TILE = 128
ROW_TILES = 64
COL_TILES = 8


def delta_matrix(tile_ids, tile_delta):
    tile_rows = tile_ids // COL_TILES
    tile_cols = tile_ids % COL_TILES
    field = jnp.zeros((ROW_TILES, TILE, COL_TILES, TILE), tile_delta.dtype)
    field = field.at[tile_rows, :, tile_cols, :].set(tile_delta)
    return field.reshape(ROW_TILES * TILE, COL_TILES * TILE)


def whole_field(all_ids, tile_delta):
    all_deltas = lax.all_gather(tile_delta, "dp", axis=0, tiled=True)
    return delta_matrix(all_ids, all_deltas)


def body(layer_input, grad_values, base_weight, tile_ids, tile_delta):
    all_ids = lax.all_gather(tile_ids, "dp", axis=0, tiled=True)
    own_rows = base_weight.shape[0]
    field = whole_field(all_ids, tile_delta)
    first_row = lax.axis_index("dp") * own_rows
    own_field = lax.dynamic_slice_in_dim(field, first_row, own_rows, 0)
    merged = (base_weight.astype(jnp.float32) + own_field.astype(jnp.float32)).astype(jnp.bfloat16)
    grad_input = lax.dot_general(
        grad_values,
        lax.all_gather(merged, "dp", axis=0, tiled=True),
        (((1,), (1,)), ((), ())),
        preferred_element_type=jnp.float32,
    ).astype(jnp.bfloat16)
    tokens_here = layer_input.shape[0]
    input_panels = layer_input.reshape(tokens_here, ROW_TILES, TILE)
    grad_panels = grad_values.reshape(tokens_here, COL_TILES, TILE)
    rows_taken = jnp.take(input_panels, all_ids // COL_TILES, axis=1)
    cols_taken = jnp.take(grad_panels, all_ids % COL_TILES, axis=1)
    summed = lax.psum_scatter(
        jnp.einsum("tja,tjb->jab", rows_taken, cols_taken, preferred_element_type=jnp.float32),
        "dp",
        scatter_dimension=0,
        tiled=True,
    )
    factor = 1.0 / math.sqrt(tokens_here * lax.axis_size("dp"))
    return (grad_input, summed * factor)


def solution(mesh):
    placed = (
        P(("groups", "dp"), None),
        P(("groups", "dp"), None),
        P("dp", None),
        P(("groups", "dp")),
        P(("groups", "dp"), None, None),
    )
    return jax.shard_map(
        body,
        mesh=mesh,
        in_specs=placed,
        out_specs=(P(("groups", "dp"), None), P(("groups", "dp"), None, None)),
        check_vma=False,
    )
```

profile of v0, /device:TPU:0, one launch (start us, length us, event | category | flops | bytes accessed | tf_op | source)
XLA Modules:
  0.0 252.2 jit_solution(3247052467888750626)
XLA Ops:
  7.2 0.0 copy-start.2
  7.2 0.0 reduce-scatter.2.cloned.1.call-start
  7.9 1.2 dynamic-slice
  9.1 0.8 dynamic-update-slice
  9.9 13.8 %all-reduce = s32[16]{0:T(128)S(1)} all-reduce(s32[16]{0:T(128)S(1)} %dynamic-update-slice), channel_id=1, replica_groups=mesh['groups'=2,'dp'=16] {'dp'}, use_global_device_ids=true, to_apply=%add | all-reduce | flops 16 | bytes 128
  23.6 1.2 copy.22
  24.9 0.3 copy.23
  25.2 6.4 %copy.20 = bf16[256,8192]{0,1:T(8,128)(2,1)} copy(bf16[256,8192]{1,0:T(8,128)(2,1)} %param.5) | data formatting | bytes 8388608 | tf_op args[0]
  31.5 6.4 %copy.21 = bf16[256,64,128]{2,0,1:T(8,128)(2,1)} copy(bf16[256,64,128]{0,2,1:T(8,128)(2,1)} %bitcast.30) | data formatting | bytes 8388608 | tf_op jit(solution)/shard_map/reshape | solution.py:39
  37.9 0.7 gather_fusion.1
  38.7 2.9 %gather_fusion = bf16[16,256,128]{2,1,0:T(8,128)(2,1)S(1)} fusion(bf16[256,64,128]{2,0,1:T(8,128)(2,1)} %copy.21, s32[1024]{0:T(1024)S(1)} %get-tuple-element.17), kind=kCustom, calls=%fused_computation | custom fusion | bytes 2097216 | tf_op jit(solution)/shard_map/jit(_take)/gather | solution.py:41
  41.6 1.5 fusion.1
  43.2 0.0 reduce-scatter.2.cloned.1.call-update
  43.2 0.0 all-gather.2.cloned.1.call-start
  43.3 0.0 copy-done.2
  43.3 19.4 %all_gather.10 = bf16[16,128,128]{2,1,0:T(8,128)(2,1)S(1)} all-gather(bf16[1,128,128]{2,1,0:T(8,128)(2,1)S(1)} %copy-done.2), channel_id=1, replica_groups=mesh['groups'=2,'dp'=16] {'dp'}, dimensions={0}, use_global_device_ids=true | all-gather | bytes 557056 | tf_op jit(solution)/shard_map/all_gather | solution.py:21
  62.6 6.3 %broadcast_in_dim.27 = bf16[64,128,8,128]{3,1,2,0:T(8,128)(2,1)} broadcast(bf16[]{:T(256)} %constant.62.clone.1), dimensions={} | broadcast | bytes 16777218 | tf_op jit(solution)/shard_map/broadcast_in_dim | solution.py:15
  69.0 2.8 %scatter_fusion = bf16[64,128,8,128]{3,1,2,0:T(8,128)(2,1)} fusion(bf16[64,128,8,128]{3,1,2,0:T(8,128)(2,1)} %broadcast_in_dim.27, s32[16]{0:T(128)S(1)} %fusion.10, bf16[16,128,128]{2,1,0:T(8,128)(2,1)S(1)} %all_gather.10), kind=kCustom, calls=%fused_computation.2 | custom fusion | bytes 1572992 | tf_op jit(solution)/shard_map/scatter | solution.py:16
  71.7 16.8 %copy.19 = bf16[64,128,8,128]{3,2,1,0:T(8,128)(2,1)S(1)} copy(bf16[64,128,8,128]{3,1,2,0:T(8,128)(2,1)} %scatter_fusion) | data formatting | bytes 33554432 | tf_op jit(solution)/shard_map/scatter | solution.py:16
  88.6 0.0 copy-start
  88.6 0.0 copy-start.1
  88.6 9.1 %copy.29 = bf16[1024,8,8,128]{3,1,2,0:T(8,128)(2,1)} copy(bf16[1024,8,8,128]{3,2,1,0:T(8,128)(2,1)S(1)} %bitcast.28) | data formatting | bytes 33554432
  97.7 0.0 copy-done
  97.7 2.6 %add_convert_fusion = bf16[512,1024]{1,0:T(8,128)(2,1)} fusion(bf16[512,1024]{1,0:T(8,128)(2,1)S(1)} %copy-done, bf16[8192,1024]{1,0:T(8,128)(2,1)} %bitcast.29, s32[]{:T(128)S(6)} %select_n.40), kind=kLoop, calls=%fused_computation.6 | loop fusion | flops 2097152 | bytes 3145732 | tf_op jit(solution)/shard_map/convert_element_type | solution.py:31
  100.3 0.0 all-gather.2.cloned.1.call-update
  100.3 0.0 reduce-scatter.2.cloned.1.call-done
  100.4 1.5 broadcast_multiply_fusion
  101.8 124.9 %all-gather.2.cloned.1.call-done = bf16[8192,1024]{1,0:T(8,128)(2,1)} async-done(((bf16[512,1024]{1,0:T(8,128)(2,1)}), bf16[8192,1024]{1,0:T(8,128)(2,1)}) %all-gather.2.cloned.1.call-update) | async-done | bytes 16777232 | tf_op jit(solution)/shard_map/all_gather | solution.py:34
  226.7 0.0 copy-done.1
  226.7 12.3 %fusion = bf16[256,8192]{0,1:T(8,128)(2,1)} fusion(bf16[8192,1024]{1,0:T(8,128)(2,1)} %all-gather.2.cloned.1.call-done, bf16[256,1024]{1,0:T(8,128)(2,1)S(1)} %copy-done.1), kind=kOutput, calls=%fused_computation.5 | convolution fusion | flops 4297064448 | bytes 21495808 | tf_op jit(solution)/shard_map/dot_general | solution.py:32
  239.0 6.3 %copy.25 = bf16[256,8192]{1,0:T(8,128)(2,1)} copy(bf16[256,8192]{0,1:T(8,128)(2,1)} %fusion) | data formatting | bytes 8388608
  (4 shorter events, 0.0 us)
Async XLA Ops:
  7.2 36.1 %copy-start.2 = (bf16[1,128,128]{2,1,0:T(8,128)(2,1)S(1)}, bf16[1,128,128]{2,1,0:T(8,128)(2,1)}, u32[]{:S(2)}) copy-start(bf16[1,128,128]{2,1,0:T(8,128)(2,1)} %param.9) | copy-start | bytes 98308
  7.2 93.2 %reduce-scatter.2.cloned.1.call-start = ((), (), s32[]{:S(2)}) async-start(), calls=%async_computation.2 | async-start | bytes 1114112 | tf_op jit(solution)/shard_map/reduce_scatter | solution.py:43
  43.2 183.5 %all-gather.2.cloned.1.call-start = ((), (), s32[]{:S(2)}) async-start(), calls=%async_computation.1 | async-start | bytes 17825792 | tf_op jit(solution)/shard_map/all_gather | solution.py:34
  88.6 9.1 %copy-start = (bf16[512,1024]{1,0:T(8,128)(2,1)S(1)}, bf16[512,1024]{1,0:T(8,128)(2,1)}, u32[]{:S(2)}) copy-start(bf16[512,1024]{1,0:T(8,128)(2,1)} %param.7) | copy-start | bytes 3145732
  88.6 138.2 %copy-start.1 = (bf16[256,1024]{1,0:T(8,128)(2,1)S(1)}, bf16[256,1024]{1,0:T(8,128)(2,1)}, u32[]{:S(2)}) copy-start(bf16[256,1024]{1,0:T(8,128)(2,1)} %param.6) | copy-start | bytes 1572868
Sparse Core Ops, SparseCore 0:
  43.3 55.1 reduce-scatter.1
  101.3 125.3 all-gather.1
where the time goes:
time: 253 us; the launch traced here: 252 us
  waiting for transfers between devices  125 us (49%)
  local copies, waits for them, and re-layouts  61.3 us (24%)
  blocking collectives  33.1 us (13%)
  between operations  14.8 us (6%)
  matrix products  13.8 us (5%)
  other arithmetic  4.11 us (2%)
    all_gather x1, waiting for transfers between devices, body(): lax.all_gather(merged, 'dp', axis=0, tiled=True)  125 us
    unnamed x13, local copies, waits for them, and re-layouts  25.1 us
    scatter x2, local copies, waits for them, and re-layouts, delta_matrix(): field = field.at[tile_rows, :, tile_cols, :].set(tile_delta)  19.6 us
    all_gather x1, blocking collectives, whole_field(): all_deltas = lax.all_gather(tile_delta, 'dp', axis=0, tiled=True)  19.4 us
    unnamed x1, blocking collectives  13.8 us
    dot_general x1, matrix products, body(): lax.dot_general(grad_values, lax.all_gather(merged, 'dp', axis=0, tiled=T...  12.3 us
    reshape x1, local copies, waits for them, and re-layouts, body(): input_panels = layer_input.reshape(tokens_here, ROW_TILES, TILE)  6.37 us
    broadcast_in_dim x1, local copies, waits for them, and re-layouts, delta_matrix(): field = jnp.zeros((ROW_TILES, TILE, COL_TILES, TILE), tile_delta.dtype)  6.31 us
  transfers between devices with their start and end apart: 2, of which 1 were waited for; matrix products, arithmetic and copies ran while one was open for 16% of the time, Pallas kernels for 0%

commit v1 on v0

--- a/solution.py
+++ b/solution.py
@@ -3,10 +3,20 @@
 import jax.numpy as jnp
 from jax import lax
 from jax.sharding import PartitionSpec as P
+from jax.lax import axis_index, ppermute, psum
 
 TILE = 128
 ROW_TILES = 64
 COL_TILES = 8
+
+
+def hold_the_islands(row_data, d_out):
+    row_data = jnp.moveaxis(row_data, 0, d_out)
+    carry_out = row_data.shape
+    reply = row_data.reshape(
+        *carry_out[:d_out], carry_out[d_out] * carry_out[d_out + 1], *carry_out[d_out + 2 :]
+    )
+    return reply
 
 
 def delta_matrix(tile_ids, tile_delta):
@@ -23,6 +33,30 @@
 
 
 def body(layer_input, grad_values, base_weight, tile_ids, tile_delta):
+
+    def unit_set(content, dim_at, lane_axis):
+        num_devices = psum(1, axis_name=lane_axis)
+        by_rank = [(k0, (k0 + 1) % num_devices) for k0 in range(num_devices)]
+        stack_in = [(s, i0) for i0, s in by_rank]
+        then, arr_now = ([], [])
+        for kk in [*range(num_devices - 1)]:
+            if kk % 2 == 0:
+                then.append(
+                    ppermute(then[-1] if then else content, perm=by_rank, axis_name=lane_axis)
+                )
+            else:
+                s_next = ppermute(
+                    arr_now[-1] if arr_now else content, axis_name=lane_axis, perm=stack_in
+                )
+                arr_now.append(s_next)
+        arr_next = jnp.stack([*then[::-1], content, *arr_now], 0)
+        x_now = axis_index(lane_axis)
+        local_now = len(then)
+        spare = x_now - local_now
+        arr_next = arr_next[(jnp.arange(num_devices) - spare) % num_devices]
+        carry = hold_the_islands(arr_next, dim_at)
+        return carry
+
     all_ids = lax.all_gather(tile_ids, "dp", axis=0, tiled=True)
     own_rows = base_weight.shape[0]
     field = whole_field(all_ids, tile_delta)
@@ -31,7 +65,7 @@
     merged = (base_weight.astype(jnp.float32) + own_field.astype(jnp.float32)).astype(jnp.bfloat16)
     grad_input = lax.dot_general(
         grad_values,
-        lax.all_gather(merged, "dp", axis=0, tiled=True),
+        unit_set(merged, 0, "dp"),
         (((1,), (1,)), ((), ())),
         preferred_element_type=jnp.float32,
     ).astype(jnp.bfloat16)

time: 253 us -> 357 us (1.41)
  starting transfers between devices: 0.08 us -> 115 us
  waiting for transfers between devices: 125 us -> 67.1 us
  local copies, waits for them, and re-layouts: 61.3 us -> 108 us
    all_gather x1 -> x0, waiting for transfers between devices: 125 us -> none  [body(): lax.all_gather(merged, 'dp', axis=0, tiled=True)]
    ppermute x0 -> x15, starting transfers between devices: none -> 115 us  [the longest x8 105 us: unit_set(): ppermute(then[-1] if then else content, perm=by_rank, axis_name=lane_axis)]
    ppermute x0 -> x15, waiting for transfers between devices: none -> 35.9 us  [the longest x8 34.2 us: unit_set(): ppermute(then[-1] if then else content, perm=by_rank, axis_name=lane_axis)]
    unnamed x13 -> x42, local copies, waits for them, and re-layouts: 25.1 us -> 56.6 us
    reduce_scatter x1, waiting for transfers between devices: 0.02 us -> 31.2 us  [body(): lax.psum_scatter(jnp.einsum('tja,tjb->jab', rows_taken, cols_taken, prefe...]
    gather x0 -> x1, local copies, waits for them, and re-layouts: none -> 13 us  [unit_set(): arr_next = arr_next[(jnp.arange(num_devices) - spare) % num_devices]]
  transfers between devices with their start and end apart: 2 -> 16, of which waited for: 1 -> 8; matrix products, arithmetic and copies ran while one was open for 16% -> 15% of each run, Pallas kernels for 0% -> 0%
where the time goes in v1:
time: 357 us; the launch traced here: 356 us
  starting transfers between devices  115 us (32%)
  local copies, waits for them, and re-layouts  108 us (30%)
  waiting for transfers between devices  67.1 us (19%)
  blocking collectives  33.4 us (9%)
  matrix products  15.1 us (4%)
  between operations  14.8 us (4%)
    ppermute x8, starting transfers between devices, unit_set(): ppermute(then[-1] if then else content, perm=by_rank, axis_name=lane_axis)  105 us
    unnamed x42, local copies, waits for them, and re-layouts  56.6 us
    ppermute x8, waiting for transfers between devices, unit_set(): ppermute(then[-1] if then else content, perm=by_rank, axis_name=lane_axis)  34.2 us
    reduce_scatter x1, waiting for transfers between devices, body(): lax.psum_scatter(jnp.einsum('tja,tjb->jab', rows_taken, cols_taken, prefe...  31.2 us
    all_gather x1, blocking collectives, whole_field(): all_deltas = lax.all_gather(tile_delta, 'dp', axis=0, tiled=True)  19.6 us
    scatter x2, local copies, waits for them, and re-layouts, delta_matrix(): field = field.at[tile_rows, :, tile_cols, :].set(tile_delta)  19.6 us
    unnamed x1, blocking collectives  13.8 us
    gather x1, local copies, waits for them, and re-layouts, unit_set(): arr_next = arr_next[(jnp.arange(num_devices) - spare) % num_devices]  13 us
  transfers between devices with their start and end apart: 16, of which 8 were waited for; matrix products, arithmetic and copies ran while one was open for 15% of the time, Pallas kernels for 0%

profile of v1, /device:TPU:0, one launch (start us, length us, event | category | flops | bytes accessed | tf_op | source)
XLA Modules:
  0.0 356.1 jit_solution(1918013126425023715)
XLA Ops:
  7.2 0.0 reduce-scatter.2.cloned.1.call-start
  7.9 1.2 dynamic-slice
  9.1 0.8 dynamic-update-slice
  9.9 13.8 %all-reduce = s32[16]{0:T(128)S(1)} all-reduce(s32[16]{0:T(128)S(1)} %dynamic-update-slice), channel_id=1, replica_groups=mesh['groups'=2,'dp'=16] {'dp'}, use_global_device_ids=true, to_apply=%add | all-reduce | flops 16 | bytes 128
  23.6 19.6 %all_gather.7 = bf16[16,128,128]{2,1,0:T(8,128)(2,1)S(1)} all-gather(bf16[1,128,128]{2,1,0:T(8,128)(2,1)} %param.9), channel_id=1, replica_groups=mesh['groups'=2,'dp'=16] {'dp'}, dimensions={0}, use_global_device_ids=true | all-gather | bytes 557056 | tf_op jit(solution)/shard_map/all_gather | solution.py:31
  43.3 6.3 %broadcast_in_dim.28 = bf16[64,128,8,128]{3,1,2,0:T(8,128)(2,1)} broadcast(bf16[]{:T(256)} %constant.73.clone.1), dimensions={} | broadcast | bytes 16777218 | tf_op jit(solution)/shard_map/broadcast_in_dim | solution.py:25
  49.6 2.8 scatter_fusion
  52.4 16.8 %copy.19 = bf16[64,128,8,128]{3,2,1,0:T(8,128)(2,1)S(1)} copy(bf16[64,128,8,128]{3,1,2,0:T(8,128)(2,1)} %scatter_fusion) | data formatting | bytes 33554432 | tf_op jit(solution)/shard_map/scatter | solution.py:26
  69.2 0.0 copy-start
  69.2 9.1 %copy.29 = bf16[1024,8,8,128]{3,1,2,0:T(8,128)(2,1)} copy(bf16[1024,8,8,128]{3,2,1,0:T(8,128)(2,1)S(1)} %bitcast.63) | data formatting | bytes 33554432
  78.4 1.7 add_convert_fusion
  80.1 0.4 collective-permute-start
  80.5 16.6 %collective-permute-done = bf16[512,1024]{1,0:T(8,128)(2,1)S(1)} collective-permute-done((bf16[512,1024]{1,0:T(8,128)(2,1)S(1)}, bf16[512,1024]{1,0:T(8,128)(2,1)S(1)}, u32[]{:S(2)}, u32[]{:S(2)}) %collective-permute-start) | collective-permute-done | bytes 1048608 | tf_op jit(solution)/shard_map/ppermute | solution.py:45
  97.0 0.0 collective-permute-start.1
  97.0 4.4 %collective-permute-start.8 = (bf16[512,1024]{1,0:T(8,128)(2,1)S(1)}, bf16[512,1024]{1,0:T(8,128)(2,1)S(1)}, u32[]{:S(2)}, u32[]{:S(2)}) collective-permute-start(bf16[512,1024]{1,0:T(8,128)(2,1)S(1)} %add_convert_fusion), channel_id=1, source_target_pairs={{1,0},{2,1},{3,2},{4,3},{5,4},{6,5},{7,6},{8,7},{9,8},{10,9},{11,1... | collective-permute-start | bytes 3145736 | tf_op jit(solution)/shard_map/ppermute | solution.py:48
  101.5 12.6 %collective-permute-done.1 = bf16[512,1024]{1,0:T(8,128)(2,1)S(1)} collective-permute-done((bf16[512,1024]{1,0:T(8,128)(2,1)S(1)}, bf16[512,1024]{1,0:T(8,128)(2,1)S(1)}, u32[]{:S(2)}, u32[]{:S(2)}) %collective-permute-start.1) | collective-permute-done | bytes 1048608 | tf_op jit(solution)/shard_map/ppermute | solution.py:45
  114.1 15.8 %collective-permute-start.2 = (bf16[512,1024]{1,0:T(8,128)(2,1)S(1)}, bf16[512,1024]{1,0:T(8,128)(2,1)S(1)}, u32[]{:S(2)}, u32[]{:S(2)}) collective-permute-start(bf16[512,1024]{1,0:T(8,128)(2,1)S(1)} %collective-permute-done.1), channel_id=1, source_target_pairs={{0,1},{1,2},{2,3},{3,4},{4,5},{5,6},{6,7},{7,8},{8,9},{9,10},{10,1... | collective-permute-start | bytes 3145736 | tf_op jit(solution)/shard_map/ppermute | solution.py:45
  129.8 0.1 collective-permute-start.9
  129.9 0.9 copy-done.2
  130.8 1.3 collective-permute-done.2
  132.1 23.2 %collective-permute-start.3 = (bf16[512,1024]{1,0:T(8,128)(2,1)S(1)}, bf16[512,1024]{1,0:T(8,128)(2,1)S(1)}, u32[]{:S(2)}, u32[]{:S(2)}) collective-permute-start(bf16[512,1024]{1,0:T(8,128)(2,1)S(1)} %collective-permute-done.2), channel_id=1, source_target_pairs={{0,1},{1,2},{2,3},{3,4},{4,5},{5,6},{6,7},{7,8},{8,9},{9,10},{10,1... | collective-permute-start | bytes 3145736 | tf_op jit(solution)/shard_map/ppermute | solution.py:45
  155.3 0.0 collective-permute-done.9
  155.3 0.1 collective-permute-start.10
  155.3 0.9 copy-done.5
  156.3 1.3 collective-permute-done.3
  157.6 23.2 %collective-permute-start.4 = (bf16[512,1024]{1,0:T(8,128)(2,1)S(1)}, bf16[512,1024]{1,0:T(8,128)(2,1)}, u32[]{:S(2)}, u32[]{:S(2)}) collective-permute-start(bf16[512,1024]{1,0:T(8,128)(2,1)S(1)} %collective-permute-done.3), channel_id=1, source_target_pairs={{0,1},{1,2},{2,3},{3,4},{4,5},{5,6},{6,7},{7,8},{8,9},{9,10},{10,1... | collective-permute-start | bytes 3145736 | tf_op jit(solution)/shard_map/ppermute | solution.py:45
  180.7 0.0 collective-permute-done.10
  180.8 2.4 collective-permute-done.4
  183.2 11.8 %collective-permute-start.5 = (bf16[512,1024]{1,0:T(8,128)(2,1)}, bf16[512,1024]{1,0:T(8,128)(2,1)}, u32[]{:S(2)}, u32[]{:S(2)}) collective-permute-start(bf16[512,1024]{1,0:T(8,128)(2,1)} %collective-permute-done.4), channel_id=1, source_target_pairs={{0,1},{1,2},{2,3},{3,4},{4,5},{5,6},{6,7},{7,8},{8,9},{9,10},{10,1... | collective-permute-start | bytes 3145736 | tf_op jit(solution)/shard_map/ppermute | solution.py:45
  195.0 6.4 %copy.20 = bf16[256,8192]{0,1:T(8,128)(2,1)} copy(bf16[256,8192]{1,0:T(8,128)(2,1)} %param.5) | data formatting | bytes 8388608 | tf_op args[0]
  201.3 6.4 %copy.21 = bf16[256,64,128]{2,0,1:T(8,128)(2,1)} copy(bf16[256,64,128]{0,2,1:T(8,128)(2,1)} %bitcast.66) | data formatting | bytes 8388608 | tf_op jit(solution)/shard_map/reshape | solution.py:73
  207.7 0.2 copy.22
  207.9 0.3 copy.23
  208.2 2.9 gather_fusion.1
  211.1 1.7 gather_fusion.2
  212.8 8.1 %collective-permute-start.6 = (bf16[512,1024]{1,0:T(8,128)(2,1)}, bf16[512,1024]{1,0:T(8,128)(2,1)}, u32[]{:S(2)}, u32[]{:S(2)}) collective-permute-start(bf16[512,1024]{1,0:T(8,128)(2,1)} %collective-permute-done.5), channel_id=1, source_target_pairs={{0,1},{1,2},{2,3},{3,4},{4,5},{5,6},{6,7},{7,8},{8,9},{9,10},{10,1... | collective-permute-start | bytes 3145736 | tf_op jit(solution)/shard_map/ppermute | solution.py:45
  220.8 2.8 fusion.1
  223.6 0.0 reduce-scatter.2.cloned.1.call-update
  223.7 1.7 collective-permute-done.12
  225.4 4.7 %collective-permute-start.13 = (bf16[512,1024]{1,0:T(8,128)(2,1)}, bf16[512,1024]{1,0:T(8,128)(2,1)}, u32[]{:S(2)}, u32[]{:S(2)}) collective-permute-start(bf16[512,1024]{1,0:T(8,128)(2,1)} %collective-permute-done.12), channel_id=1, source_target_pairs={{1,0},{2,1},{3,2},{4,3},{5,4},{6,5},{7,6},{8,7},{9,8},{10,9},{11,1... | collective-permute-start | bytes 3145736 | tf_op jit(solution)/shard_map/ppermute | solution.py:48
  230.1 0.1 collective-permute-done.6
  230.2 22.9 %collective-permute-start.7 = (bf16[512,1024]{1,0:T(8,128)(2,1)}, bf16[512,1024]{1,0:T(8,128)(2,1)}, u32[]{:S(2)}, u32[]{:S(2)}) collective-permute-start(bf16[512,1024]{1,0:T(8,128)(2,1)} %collective-permute-done.6), channel_id=1, source_target_pairs={{0,1},{1,2},{2,3},{3,4},{4,5},{5,6},{6,7},{7,8},{8,9},{9,10},{10,1... | collective-permute-start | bytes 3145736 | tf_op jit(solution)/shard_map/ppermute | solution.py:45
  253.1 31.2 %reduce-scatter.2.cloned.1.call-done = f32[1,128,128]{2,1,0:T(8,128)} async-done(((f32[16,128,128]{2,1,0:T(8,128)}), f32[1,128,128]{2,1,0:T(8,128)}) %reduce-scatter.2.cloned.1.call-update) | async-done | bytes 65552 | tf_op jit(solution)/shard_map/reduce_scatter | solution.py:77
  284.3 1.6 broadcast_multiply_fusion
  285.8 0.1 collective-permute-start.14
  285.9 2.3 bitcast_dynamic-update-slice_fusion.15
  288.2 2.3 bitcast_dynamic-update-slice_fusion.14
  290.5 2.3 bitcast_dynamic-update-slice_fusion.13
  292.7 2.3 bitcast_dynamic-update-slice_fusion.12
  295.0 2.3 bitcast_dynamic-update-slice_fusion.11
  297.3 2.3 bitcast_dynamic-update-slice_fusion.10
  299.6 2.3 bitcast_dynamic-update-slice_fusion.9
  301.8 2.3 bitcast_dynamic-update-slice_fusion.8
  304.2 1.1 bitcast_dynamic-update-slice_fusion.7
  305.3 1.1 bitcast_dynamic-update-slice_fusion.6
  306.4 1.0 bitcast_dynamic-update-slice_fusion.5
  307.4 2.3 bitcast_dynamic-update-slice_fusion.4
  309.7 2.3 bitcast_dynamic-update-slice_fusion.3
  312.0 2.3 bitcast_dynamic-update-slice_fusion.2
  314.3 2.3 bitcast_dynamic-update-slice_fusion.1
  316.6 1.0 bitcast_dynamic-update-slice_fusion
  317.6 13.0 %gather_fusion = bf16[16,512,1024]{2,1,0:T(8,128)(2,1)} fusion(bf16[16,512,1024]{2,1,0:T(8,128)(2,1)} %bitcast_dynamic-update-slice_fusion, s32[1024]{0:T(1024)S(1)} %pad_clamp_fusion.2), kind=kCustom, calls=%fused_computation | custom fusion | bytes 33554496 | tf_op jit(solution)/shard_map/gather | solution.py:56
  330.7 12.3 %fusion = bf16[256,8192]{0,1:T(8,128)(2,1)} fusion(bf16[8192,1024]{1,0:T(8,128)(2,1)} %bitcast.65, bf16[256,1024]{1,0:T(8,128)(2,1)S(1)} %copy-done.9), kind=kOutput, calls=%fused_computation.6 | convolution fusion | flops 4297064448 | bytes 21495808 | tf_op jit(solution)/shard_map/dot_general | solution.py:66
  343.0 6.3 %copy.25 = bf16[256,8192]{1,0:T(8,128)(2,1)} copy(bf16[256,8192]{0,1:T(8,128)(2,1)} %fusion) | data formatting | bytes 8388608
  (31 shorter events, 0.1 us)
Async XLA Ops:
  7.2 277.1 %reduce-scatter.2.cloned.1.call-start = ((), (), s32[]{:S(2)}) async-start(), calls=%async_computation.1 | async-start | bytes 1114112 | tf_op jit(solution)/shard_map/reduce_scatter | solution.py:77
  69.2 9.1 %copy-start = (bf16[512,1024]{1,0:T(8,128)(2,1)S(1)}, bf16[512,1024]{1,0:T(8,128)(2,1)}, u32[]{:S(2)}) copy-start(bf16[512,1024]{1,0:T(8,128)(2,1)} %param.7) | copy-start | bytes 3145732
  78.4 129.3 %copy-start.9 = (bf16[256,1024]{1,0:T(8,128)(2,1)S(1)}, bf16[256,1024]{1,0:T(8,128)(2,1)}, u32[]{:S(2)}) copy-start(bf16[256,1024]{1,0:T(8,128)(2,1)} %param.6) | copy-start | bytes 1572868
  80.1 17.0 %collective-permute-start = (bf16[512,1024]{1,0:T(8,128)(2,1)S(1)}, bf16[512,1024]{1,0:T(8,128)(2,1)S(1)}, u32[]{:S(2)}, u32[]{:S(2)}) collective-permute-start(bf16[512,1024]{1,0:T(8,128)(2,1)S(1)} %add_convert_fusion), channel_id=1, source_target_pairs={{0,1},{1,2},{2,3},{3,4},{4,5},{5,6},{6,7},{7,8},{8,9},{9,10},{10,1... | collective-permute-start | bytes 3145736 | tf_op jit(solution)/shard_map/ppermute | solution.py:45
  97.0 32.8 %copy-start.1 = (bf16[512,1024]{1,0:T(8,128)(2,1)}, bf16[512,1024]{1,0:T(8,128)(2,1)S(1)}, u32[]{:S(2)}) copy-start(bf16[512,1024]{1,0:T(8,128)(2,1)S(1)} %collective-permute-done) | copy-start | bytes 3145732
  97.0 17.0 %collective-permute-start.1 = (bf16[512,1024]{1,0:T(8,128)(2,1)S(1)}, bf16[512,1024]{1,0:T(8,128)(2,1)S(1)}, u32[]{:S(2)}, u32[]{:S(2)}) collective-permute-start(bf16[512,1024]{1,0:T(8,128)(2,1)S(1)} %collective-permute-done), channel_id=1, source_target_pairs={{0,1},{1,2},{2,3},{3,4},{4,5},{5,6},{6,7},{7,8},{8,9},{9,10},{10,1... | collective-permute-start | bytes 3145736 | tf_op jit(solution)/shard_map/ppermute | solution.py:45
  97.0 32.8 %collective-permute-start.8 = (bf16[512,1024]{1,0:T(8,128)(2,1)S(1)}, bf16[512,1024]{1,0:T(8,128)(2,1)S(1)}, u32[]{:S(2)}, u32[]{:S(2)}) collective-permute-start(bf16[512,1024]{1,0:T(8,128)(2,1)S(1)} %add_convert_fusion), channel_id=1, source_target_pairs={{1,0},{2,1},{3,2},{4,3},{5,4},{6,5},{7,6},{8,7},{9,8},{10,9},{11,1... | collective-permute-start | bytes 3145736 | tf_op jit(solution)/shard_map/ppermute | solution.py:48
  114.1 41.2 %copy-start.4 = (bf16[512,1024]{1,0:T(8,128)(2,1)}, bf16[512,1024]{1,0:T(8,128)(2,1)S(1)}, u32[]{:S(2)}) copy-start(bf16[512,1024]{1,0:T(8,128)(2,1)S(1)} %collective-permute-done.1) | copy-start | bytes 3145732
  114.1 18.0 %collective-permute-start.2 = (bf16[512,1024]{1,0:T(8,128)(2,1)S(1)}, bf16[512,1024]{1,0:T(8,128)(2,1)S(1)}, u32[]{:S(2)}, u32[]{:S(2)}) collective-permute-start(bf16[512,1024]{1,0:T(8,128)(2,1)S(1)} %collective-permute-done.1), channel_id=1, source_target_pairs={{0,1},{1,2},{2,3},{3,4},{4,5},{5,6},{6,7},{7,8},{8,9},{9,10},{10,1... | collective-permute-start | bytes 3145736 | tf_op jit(solution)/shard_map/ppermute | solution.py:45
  129.8 1.0 copy-start.2
  129.8 25.5 %collective-permute-start.9 = (bf16[512,1024]{1,0:T(8,128)(2,1)S(1)}, bf16[512,1024]{1,0:T(8,128)(2,1)S(1)}, u32[]{:S(2)}, u32[]{:S(2)}) collective-permute-start(bf16[512,1024]{1,0:T(8,128)(2,1)S(1)} %collective-permute-done.8), channel_id=1, source_target_pairs={{1,0},{2,1},{3,2},{4,3},{5,4},{6,5},{7,6},{8,7},{9,8},{10,9},{11,1... | collective-permute-start | bytes 3145736 | tf_op jit(solution)/shard_map/ppermute | solution.py:48
  132.1 48.6 %copy-start.7 = (bf16[512,1024]{1,0:T(8,128)(2,1)}, bf16[512,1024]{1,0:T(8,128)(2,1)S(1)}, u32[]{:S(2)}) copy-start(bf16[512,1024]{1,0:T(8,128)(2,1)S(1)} %collective-permute-done.2) | copy-start | bytes 3145732
  132.1 25.5 %collective-permute-start.3 = (bf16[512,1024]{1,0:T(8,128)(2,1)S(1)}, bf16[512,1024]{1,0:T(8,128)(2,1)S(1)}, u32[]{:S(2)}, u32[]{:S(2)}) collective-permute-start(bf16[512,1024]{1,0:T(8,128)(2,1)S(1)} %collective-permute-done.2), channel_id=1, source_target_pairs={{0,1},{1,2},{2,3},{3,4},{4,5},{5,6},{6,7},{7,8},{8,9},{9,10},{10,1... | collective-permute-start | bytes 3145736 | tf_op jit(solution)/shard_map/ppermute | solution.py:45
  155.3 1.0 copy-start.5
  155.3 25.5 %collective-permute-start.10 = (bf16[512,1024]{1,0:T(8,128)(2,1)S(1)}, bf16[512,1024]{1,0:T(8,128)(2,1)}, u32[]{:S(2)}, u32[]{:S(2)}) collective-permute-start(bf16[512,1024]{1,0:T(8,128)(2,1)S(1)} %collective-permute-done.9), channel_id=1, source_target_pairs={{1,0},{2,1},{3,2},{4,3},{5,4},{6,5},{7,6},{8,7},{9,8},{10,9},{11,1... | collective-permute-start | bytes 3145736 | tf_op jit(solution)/shard_map/ppermute | solution.py:48
  157.6 23.2 %copy-start.8 = (bf16[512,1024]{1,0:T(8,128)(2,1)}, bf16[512,1024]{1,0:T(8,128)(2,1)S(1)}, u32[]{:S(2)}) copy-start(bf16[512,1024]{1,0:T(8,128)(2,1)S(1)} %collective-permute-done.3) | copy-start | bytes 3145732
  157.6 25.6 %collective-permute-start.4 = (bf16[512,1024]{1,0:T(8,128)(2,1)S(1)}, bf16[512,1024]{1,0:T(8,128)(2,1)}, u32[]{:S(2)}, u32[]{:S(2)}) collective-permute-start(bf16[512,1024]{1,0:T(8,128)(2,1)S(1)} %collective-permute-done.3), channel_id=1, source_target_pairs={{0,1},{1,2},{2,3},{3,4},{4,5},{5,6},{6,7},{7,8},{8,9},{9,10},{10,1... | collective-permute-start | bytes 3145736 | tf_op jit(solution)/shard_map/ppermute | solution.py:45
  180.7 32.0 %collective-permute-start.11 = (bf16[512,1024]{1,0:T(8,128)(2,1)}, bf16[512,1024]{1,0:T(8,128)(2,1)}, u32[]{:S(2)}, u32[]{:S(2)}) collective-permute-start(bf16[512,1024]{1,0:T(8,128)(2,1)} %collective-permute-done.10), channel_id=1, source_target_pairs={{1,0},{2,1},{3,2},{4,3},{5,4},{6,5},{7,6},{8,7},{9,8},{10,9},{11,1... | collective-permute-start | bytes 3145736 | tf_op jit(solution)/shard_map/ppermute | solution.py:48
  183.2 29.6 %collective-permute-start.5 = (bf16[512,1024]{1,0:T(8,128)(2,1)}, bf16[512,1024]{1,0:T(8,128)(2,1)}, u32[]{:S(2)}, u32[]{:S(2)}) collective-permute-start(bf16[512,1024]{1,0:T(8,128)(2,1)} %collective-permute-done.4), channel_id=1, source_target_pairs={{0,1},{1,2},{2,3},{3,4},{4,5},{5,6},{6,7},{7,8},{8,9},{9,10},{10,1... | collective-permute-start | bytes 3145736 | tf_op jit(solution)/shard_map/ppermute | solution.py:45
  212.8 12.6 %collective-permute-start.12 = (bf16[512,1024]{1,0:T(8,128)(2,1)}, bf16[512,1024]{1,0:T(8,128)(2,1)}, u32[]{:S(2)}, u32[]{:S(2)}) collective-permute-start(bf16[512,1024]{1,0:T(8,128)(2,1)} %collective-permute-done.11), channel_id=1, source_target_pairs={{1,0},{2,1},{3,2},{4,3},{5,4},{6,5},{7,6},{8,7},{9,8},{10,9},{11,1... | collective-permute-start | bytes 3145736 | tf_op jit(solution)/shard_map/ppermute | solution.py:48
  212.8 17.4 %collective-permute-start.6 = (bf16[512,1024]{1,0:T(8,128)(2,1)}, bf16[512,1024]{1,0:T(8,128)(2,1)}, u32[]{:S(2)}, u32[]{:S(2)}) collective-permute-start(bf16[512,1024]{1,0:T(8,128)(2,1)} %collective-permute-done.5), channel_id=1, source_target_pairs={{0,1},{1,2},{2,3},{3,4},{4,5},{5,6},{6,7},{7,8},{8,9},{9,10},{10,1... | collective-permute-start | bytes 3145736 | tf_op jit(solution)/shard_map/ppermute | solution.py:45
  223.6 81.7 %copy-start.3 = (bf16[512,1024]{1,0:T(8,128)(2,1)S(1)}, bf16[512,1024]{1,0:T(8,128)(2,1)}, u32[]{:S(2)}) copy-start(bf16[512,1024]{1,0:T(8,128)(2,1)} %copy-done.2) | copy-start | bytes 3145732
  225.4 60.4 %collective-permute-start.13 = (bf16[512,1024]{1,0:T(8,128)(2,1)}, bf16[512,1024]{1,0:T(8,128)(2,1)}, u32[]{:S(2)}, u32[]{:S(2)}) collective-permute-start(bf16[512,1024]{1,0:T(8,128)(2,1)} %collective-permute-done.12), channel_id=1, source_target_pairs={{1,0},{2,1},{3,2},{4,3},{5,4},{6,5},{7,6},{8,7},{9,8},{10,9},{11,1... | collective-permute-start | bytes 3145736 | tf_op jit(solution)/shard_map/ppermute | solution.py:48
  230.2 55.7 %collective-permute-start.7 = (bf16[512,1024]{1,0:T(8,128)(2,1)}, bf16[512,1024]{1,0:T(8,128)(2,1)}, u32[]{:S(2)}, u32[]{:S(2)}) collective-permute-start(bf16[512,1024]{1,0:T(8,128)(2,1)} %collective-permute-done.6), channel_id=1, source_target_pairs={{0,1},{1,2},{2,3},{3,4},{4,5},{5,6},{6,7},{7,8},{8,9},{9,10},{10,1... | collective-permute-start | bytes 3145736 | tf_op jit(solution)/shard_map/ppermute | solution.py:45
  284.3 22.1 %copy-start.6 = (bf16[512,1024]{1,0:T(8,128)(2,1)S(1)}, bf16[512,1024]{1,0:T(8,128)(2,1)}, u32[]{:S(2)}) copy-start(bf16[512,1024]{1,0:T(8,128)(2,1)} %copy-done.5) | copy-start | bytes 3145732
  285.8 30.8 %collective-permute-start.14 = (bf16[512,1024]{1,0:T(8,128)(2,1)}, bf16[512,1024]{1,0:T(8,128)(2,1)S(1)}, u32[]{:S(2)}, u32[]{:S(2)}) collective-permute-start(bf16[512,1024]{1,0:T(8,128)(2,1)} %collective-permute-done.13), channel_id=1, source_target_pairs={{1,0},{2,1},{3,2},{4,3},{5,4},{6,5},{7,6},{8,7},{9,8},{10,9},{11,1... | collective-permute-start | bytes 3145736 | tf_op jit(solution)/shard_map/ppermute | solution.py:48
Sparse Core Ops, SparseCore 0:
  223.8 60.4 reduce-scatter.1
